TPU v7x, 32 devices: a whole 2x2x4 slice. The times are simulated.
32 devices in a mesh: section: 2 (over core), dp: 16 (over z, y, x).
Axes of the slice: x: 2, y: 2, z: 4, core: 2. Of those that a mesh axis runs over, the one named last changes fastest.
Arguments:
- acts: bfloat16 [2, 16, 1, 64, 2, 2, 128], P('section', 'dp'), may hold values from -6 to 6
- preacts: bfloat16 [2, 16, 1, 64, 2, 2, 128], P('section', 'dp'), may hold values from -6 to 6
- top_grad: bfloat16 [16, 1, 64, 2, 2, 128], P('dp'), may hold values from -6 to 6
- weights: bfloat16 [2, 64, 1728], P('section'), may hold values from -0.21875 to 0.21875
- a_factor: bfloat16 [2, 1728, 1728], P('section', 'dp'), as said below
- g_factor: bfloat16 [2, 64, 64], P('section'), as said below
Outputs:
- act_grads: bfloat16 [2, 16, 1, 64, 2, 2, 128], P('section', 'dp')
- update: float32 [2, 1728, 64], P('section', 'dp')
- inverse: float32 [2, 1728, 1728], P('section', 'dp')
Inputs may be any that keep to these rules, and one draw needn't show every extreme that they name: `a_factor`: each matrix is symmetric and positive definite. `g_factor`: each matrix is symmetric and positive definite.
All inputs are finite; a program needn't handle non-finite values. Where the computation divides by a largest or mean magnitude, that divisor is 1e-20 or more.
Results may differ from a plain program's by a relative error of at most 0.006.
Values may be sent and summed in bfloat16 or wider, within the bound.
No kernel may reach another device: no remote copies, remote signals or barrier semaphores. Data moves between devices by JAX's collectives and lax.ppermute only.
A program may use at most 64 MiB of HBM per device.

v0:
```python
import jax
import jax.numpy as jnp
from jax import lax
from jax.sharding import PartitionSpec as P

KW = 3
MICRO = 1


def shifted(value, axis, steps):
    count = lax.axis_size(axis)
    first, last = (max(0, -steps), min(count, count - steps))
    return lax.ppermute(value, axis, [(source, source + steps) for source in range(first, last)])


def tap_offsets(kernel_width):
    middle = kernel_width // 2
    result = []
    for along_x in range(kernel_width):
        for along_y in range(kernel_width):
            for along_z in range(kernel_width):
                result.append((along_x - middle, along_y - middle, along_z - middle))
    return result


def taps_stack(volume, kernel_width, direction):
    middle = kernel_width // 2
    padded = jnp.pad(volume, ((0, 0), (middle, middle), (middle, middle), (middle, middle)))
    size_x, size_y, size_z = (volume.shape[1], volume.shape[2], volume.shape[3])
    pieces = []
    for off_x, off_y, off_z in tap_offsets(kernel_width):
        start_x = middle + direction * off_x
        start_y = middle + direction * off_y
        start_z = middle + direction * off_z
        pieces.append(
            padded[
                :,
                start_x : start_x + size_x,
                start_y : start_y + size_y,
                start_z : start_z + size_z,
            ]
        )
    stacked = jnp.stack(pieces, 0)
    return stacked.reshape(len(pieces) * volume.shape[0], size_x * size_y * size_z)


def back_input(grad_out, w_rows):
    columns = taps_stack(grad_out, KW, -1)
    summed = lax.dot_general(
        w_rows, columns, (((0,), (0,)), ((), ())), preferred_element_type=jnp.float32
    )
    return summed.astype(jnp.bfloat16).reshape(grad_out.shape)


def back_weight(volume, grad_out):
    columns = taps_stack(volume, KW, 1)
    flattened = grad_out.reshape(grad_out.shape[0], -1)
    return lax.dot_general(
        columns, flattened, (((1,), (1,)), ((), ())), preferred_element_type=jnp.float32
    )


def local_inverse(matrix):
    values = matrix.astype(jnp.float32)
    step_size = 1.0 / jnp.max(jnp.sum(jnp.abs(values), axis=1))
    identity = jnp.eye(matrix.shape[0], dtype=jnp.float32)
    resid0 = (identity - step_size * values).astype(jnp.bfloat16)
    resid1 = jnp.dot(resid0, resid0, preferred_element_type=jnp.float32).astype(jnp.bfloat16)
    cross_term = jnp.dot(resid1, resid0, preferred_element_type=jnp.float32)
    return step_size * (
        identity + resid0.astype(jnp.float32) + resid1.astype(jnp.float32) + cross_term
    )


def eye_rows(start_row, row_total, order_full):
    column_ids = lax.broadcasted_iota(jnp.int32, (row_total, order_full), 1)
    row_ids = lax.broadcasted_iota(jnp.int32, (row_total, order_full), 0)
    return (column_ids == start_row + row_ids).astype(jnp.float32)


def doubling_sum(value, axis):
    count = lax.axis_size(axis)
    assert count & count - 1 == 0
    stride = 1
    while stride < count:
        value = value + lax.ppermute(value, axis, [(i, i ^ stride) for i in range(count)])
        stride *= 2
    return value


def shards(acts, preacts, top_grad, weights, a_factor, g_factor):
    section_index = lax.axis_index("section")
    section_count = lax.axis_size("section")
    tick_count = MICRO + section_count - 1
    gathered = lax.all_gather(a_factor[0], "dp", axis=0, tiled=True)
    inputs = acts[0, 0]
    pre_values = preacts[0, 0]
    upper_grads = top_grad[0]
    channels = weights.shape[1]
    w_rows = weights[0].reshape(channels, -1, channels).transpose(1, 0, 2).reshape(-1, channels)
    zero_field = jnp.zeros(inputs.shape[1:], jnp.bfloat16)

    def one_tick(tick_index, carried):
        outgoing, stored_grads, stored_slopes = carried
        incoming = shifted(outgoing, "section", -1)
        micro_index = tick_index - (section_count - 1 - section_index)
        is_valid = jnp.logical_and(micro_index >= 0, micro_index < MICRO)
        clipped = jnp.clip(micro_index, 0, MICRO - 1)
        from_top = lax.dynamic_index_in_dim(upper_grads, clipped, 0, keepdims=False)
        arriving = jnp.where(section_index == section_count - 1, from_top, incoming)
        pre_now = lax.dynamic_index_in_dim(pre_values, clipped, 0, keepdims=False)
        grad_out = jnp.where(pre_now > 0, arriving, zero_field)
        sending = back_input(grad_out, w_rows)
        old_grad = lax.dynamic_index_in_dim(stored_grads, clipped, 0, keepdims=False)
        old_slope = lax.dynamic_index_in_dim(stored_slopes, clipped, 0, keepdims=False)
        stored_grads = lax.dynamic_update_index_in_dim(
            stored_grads, jnp.where(is_valid, sending, old_grad), clipped, 0
        )
        stored_slopes = lax.dynamic_update_index_in_dim(
            stored_slopes, jnp.where(is_valid, grad_out, old_slope), clipped, 0
        )
        return (sending, stored_grads, stored_slopes)

    start_state = (
        zero_field,
        jnp.zeros(inputs.shape, jnp.bfloat16),
        jnp.zeros(inputs.shape, jnp.bfloat16),
    )
    last_sent, stored_grads, stored_slopes = lax.fori_loop(0, tick_count, one_tick, start_state)
    local_grad = back_weight(inputs[0], stored_slopes[0])
    summed_grad = doubling_sum(local_grad, "dp")
    mean_grad = summed_grad / lax.axis_size("dp")
    a_rows = a_factor[0]
    row_total = a_rows.shape[0]
    order_full = a_rows.shape[1]
    first_row = lax.axis_index("dp") * row_total
    full_values = gathered.astype(jnp.float32)
    step_size = 1.0 / jnp.max(jnp.sum(jnp.abs(full_values), axis=1))
    full_resid0 = (jnp.eye(order_full, dtype=jnp.float32) - step_size * full_values).astype(
        jnp.bfloat16
    )
    own_eye = eye_rows(first_row, row_total, order_full)
    resid0 = (own_eye - step_size * a_rows.astype(jnp.float32)).astype(jnp.bfloat16)
    resid1 = jnp.dot(resid0, full_resid0, preferred_element_type=jnp.float32).astype(jnp.bfloat16)
    cross_term = jnp.dot(resid1, full_resid0, preferred_element_type=jnp.float32)
    inverse_rows = step_size * (
        own_eye + resid0.astype(jnp.float32) + resid1.astype(jnp.float32) + cross_term
    )
    g_inverse = local_inverse(g_factor[0])
    preconditioned = jnp.dot(
        mean_grad, g_inverse, precision=lax.Precision.HIGHEST, preferred_element_type=jnp.float32
    )
    update_rows = jnp.dot(
        inverse_rows,
        preconditioned,
        precision=lax.Precision.HIGHEST,
        preferred_element_type=jnp.float32,
    )
    return (stored_grads[None, None], update_rows[None], inverse_rows[None])


def solution(mesh):
    placed = (
        P("section", "dp", None, None, None, None, None),
        P("section", "dp", None, None, None, None, None),
        P("dp", None, None, None, None, None),
        P("section", None, None),
        P("section", "dp", None),
        P("section", None, None),
    )
    return jax.shard_map(
        shards,
        mesh=mesh,
        in_specs=placed,
        out_specs=(
            P("section", "dp", None, None, None, None, None),
            P("section", "dp", None),
            P("section", "dp", None),
        ),
        check_vma=False,
    )
```

profile of v0, /device:TPU:7, one launch (start us, length us, event | category | flops | bytes accessed | tf_op | source)
XLA Modules:
  0.0 239.3 jit_solution(13392514546595699222)
XLA Ops:
  7.2 2.5 %copy.17 = bf16[1,108,1728]{2,0,1:T(2,128)(2,1)} copy(bf16[1,108,1728]{2,1,0:T(8,128)(2,1)} %param.12) | data formatting | bytes 746496 | tf_op args[4]
  10.3 0.9 copy.19
  14.6 2.3 reshape.66
  16.9 0.7 broadcast.37
  17.5 0.6 broadcast.38
  18.2 24.4 %while.20 = (s32[]{:T(128)}, bf16[64,2,2,128]{3,2,1,0:T(2,128)(2,1)}, bf16[1,64,2,2,128]{4,3,2,1,0:T(2,128)(2,1)}, bf16[1,64,2,2,128]{4,3,2,1,0:T(2,128)(2,1)}, ...) while((s32[]{:T(128)}, ...), condition=%wide.region_1.2_spmd.clone, body=%wide.region_0.1_spmd.clone.sunk | while | flops 113475592 | bytes 10772739 | solution.py:129
  18.2 2.6 %collective-permute-start = (bf16[64,2,2,128]{3,2,1,0:T(2,128)(2,1)}, bf16[64,2,2,128]{3,2,1,0:T(2,128)(2,1)S(1)}, u32[]{:S(2)}, u32[]{:S(2)}) collective-permute-start(bf16[64,2,2,128]{3,2,1,0:T(2,128)(2,1)} %get-tuple-element.362), channel_id=1, source_target_pairs={{16,0},{17,1},{18,2},{19,3},{20,4},{21,5},{22,6},{23,7},{24,8},{25... | collective-permute-start | bytes 196616 | tf_op jit(solution)/shard_map/while/body/eval_jaxpr/ppermute | solution.py:13
  20.8 1.1 collective-permute-done
  21.9 1.7 fusion.172
  26.9 0.7 reshape.81
  27.7 1.5 fusion.199
  29.2 0.6 reshape.82
  30.6 2.2 collective-permute-start
  32.8 1.1 collective-permute-done
  33.9 1.7 fusion.172
  38.9 0.7 reshape.81
  39.7 1.5 fusion.199
  42.6 0.9 reshape_squeeze.7
  43.5 2.1 fusion.130
  45.9 21.8 %collective-permute-done.1 = f32[1728,64]{0,1:T(8,128)S(1)} collective-permute-done((f32[1728,64]{0,1:T(8,128)S(1)}, f32[1728,64]{0,1:T(8,128)S(1)}, u32[]{:S(2)}, u32[]{:S(2)}) %collective-permute-start.1) | collective-permute-done | bytes 442400 | tf_op jit(solution)/shard_map/ppermute | solution.py:86
  68.1 10.9 %collective-permute-done.2 = f32[1728,64]{0,1:T(8,128)S(1)} collective-permute-done((f32[1728,64]{0,1:T(8,128)S(1)}, f32[1728,64]{0,1:T(8,128)S(1)}, u32[]{:S(2)}, u32[]{:S(2)}) %collective-permute-start.2) | collective-permute-done | bytes 442400 | tf_op jit(solution)/shard_map/ppermute | solution.py:86
  79.1 1.2 collective-permute-start.3
  81.6 19.6 %collective-permute-done.3 = f32[1728,64]{0,1:T(8,128)S(1)} collective-permute-done((f32[1728,64]{0,1:T(8,128)S(1)}, f32[1728,64]{0,1:T(8,128)S(1)}, u32[]{:S(2)}, u32[]{:S(2)}) %collective-permute-start.3) | collective-permute-done | bytes 442400 | tf_op jit(solution)/shard_map/ppermute | solution.py:86
  101.3 2.3 collective-permute-start.4
  103.9 39.1 %collective-permute-done.4 = f32[1728,64]{0,1:T(8,128)S(1)} collective-permute-done((f32[1728,64]{0,1:T(8,128)S(1)}, f32[1728,64]{0,1:T(8,128)S(1)}, u32[]{:S(2)}, u32[]{:S(2)}) %collective-permute-start.4) | collective-permute-done | bytes 442400 | tf_op jit(solution)/shard_map/ppermute | solution.py:86
  143.5 48.4 %all-gather.3.cloned.1.call-done = bf16[1,1728,1728]{2,0,1:T(2,128)(2,1)} async-done(((bf16[1,108,1728]{2,0,1:T(2,128)(2,1)}), bf16[1,1728,1728]{2,0,1:T(2,128)(2,1)}) %all-gather.3.cloned.1.call-update) | async-done | bytes 5971984 | tf_op jit(solution)/shard_map/all_gather | solution.py:95
  191.9 18.9 %abs_reduce_fusion = f32[1728]{0:T(1024)S(1)} fusion(bf16[1,1728,1728]{2,0,1:T(2,128)(2,1)} %all-gather.3.cloned.1.call-done), kind=kLoop, calls=%fused_computation.89 | loop fusion | flops 8956224 | bytes 5978880 | tf_op jit(solution)/shard_map/reduce_sum | solution.py:138
  212.1 14.3 %convert_multiply_fusion = f32[1,1728,1728]{2,0,1:T(1,128)S(1)} fusion(bf16[1,1728,1728]{2,0,1:T(2,128)(2,1)} %all-gather.3.cloned.1.call-done, f32[]{:T(128)S(6)} %div.12), kind=kLoop, calls=%fused_computation.90 | loop fusion | flops 5971968 | bytes 17915908 | tf_op jit(solution)/shard_map/mul | solution.py:139
  226.5 1.3 convolution_convert_fusion.1
  227.8 1.4 fusion.55
  229.2 1.6 convolution_bitcast_fusion
  230.8 1.7 copy.18
  (118 shorter events, 15.6 us)
Async XLA Ops:
  7.2 2.7 %copy-start.4 = (bf16[1,64,1728]{2,1,0:T(8,128)(2,1)S(1)}, bf16[1,64,1728]{2,1,0:T(8,128)(2,1)}, u32[]{:S(2)}) copy-start(bf16[1,64,1728]{2,1,0:T(8,128)(2,1)} %param.11) | copy-start | bytes 663556
  7.2 4.1 %copy-start = (bf16[1,1,1,64,2,2,128]{6,5,4,3,2,1,0:T(2,128)(2,1)S(1)}, bf16[1,1,1,64,2,2,128]{6,5,4,3,2,1,0:T(2,128)(2,1)}, u32[]{:S(2)}) copy-start(bf16[1,1,1,64,2,2,128]{6,5,4,3,2,1,0:T(2,128)(2,1)} %param.8) | copy-start | bytes 196612
  7.2 184.7 %all-gather.3.cloned.1.call-start = ((), (), s32[]{:S(2)}) async-start(), calls=%async_computation | async-start | bytes 13160448 | tf_op jit(solution)/shard_map/all_gather | solution.py:95
  18.2 3.7 %collective-permute-start = (bf16[64,2,2,128]{3,2,1,0:T(2,128)(2,1)}, bf16[64,2,2,128]{3,2,1,0:T(2,128)(2,1)S(1)}, u32[]{:S(2)}, u32[]{:S(2)}) collective-permute-start(bf16[64,2,2,128]{3,2,1,0:T(2,128)(2,1)} %get-tuple-element.362), channel_id=1, source_target_pairs={{16,0},{17,1},{18,2},{19,3},{20,4},{21,5},{22,6},{23,7},{24,8},{25... | collective-permute-start | bytes 196616 | tf_op jit(solution)/shard_map/while/body/eval_jaxpr/ppermute | solution.py:13
  27.6 2.2 copy-start.2
  29.9 0.6 copy-start.3
  30.6 3.3 %collective-permute-start = (bf16[64,2,2,128]{3,2,1,0:T(2,128)(2,1)}, bf16[64,2,2,128]{3,2,1,0:T(2,128)(2,1)S(1)}, u32[]{:S(2)}, u32[]{:S(2)}) collective-permute-start(bf16[64,2,2,128]{3,2,1,0:T(2,128)(2,1)} %get-tuple-element.362), channel_id=1, source_target_pairs={{16,0},{17,1},{18,2},{19,3},{20,4},{21,5},{22,6},{23,7},{24,8},{25... | collective-permute-start | bytes 196616 | tf_op jit(solution)/shard_map/while/body/eval_jaxpr/ppermute | solution.py:13
  39.7 2.2 copy-start.2
  42.0 0.6 copy-start.3
  45.6 34.6 %copy-start.5 = (bf16[1,64,64]{2,1,0:T(8,128)(2,1)S(1)}, bf16[1,64,64]{2,1,0:T(8,128)(2,1)}, u32[]{:S(2)}) copy-start(bf16[1,64,64]{2,1,0:T(8,128)(2,1)} %param.13) | copy-start | bytes 24580
  45.6 22.1 %collective-permute-start.1 = (f32[1728,64]{0,1:T(8,128)S(1)}, f32[1728,64]{0,1:T(8,128)S(1)}, u32[]{:S(2)}, u32[]{:S(2)}) collective-permute-start(f32[1728,64]{0,1:T(8,128)S(1)} %fusion.130), channel_id=1, source_target_pairs={{0,1},{1,0},{2,3},{3,2},{4,5},{5,4},{6,7},{7,6},{8,9},{9,8},{10,11... | collective-permute-start | bytes 1327112 | tf_op jit(solution)/shard_map/ppermute | solution.py:86
  67.8 11.2 %collective-permute-start.2 = (f32[1728,64]{0,1:T(8,128)S(1)}, f32[1728,64]{0,1:T(8,128)S(1)}, u32[]{:S(2)}, u32[]{:S(2)}) collective-permute-start(f32[1728,64]{0,1:T(8,128)S(1)} %add.76), channel_id=1, source_target_pairs={{0,2},{1,3},{2,0},{3,1},{4,6},{5,7},{6,4},{7,5},{8,10},{9,11},{10,... | collective-permute-start | bytes 1327112 | tf_op jit(solution)/shard_map/ppermute | solution.py:86
  79.1 22.2 %collective-permute-start.3 = (f32[1728,64]{0,1:T(8,128)S(1)}, f32[1728,64]{0,1:T(8,128)S(1)}, u32[]{:S(2)}, u32[]{:S(2)}) collective-permute-start(f32[1728,64]{0,1:T(8,128)S(1)} %add.77), channel_id=1, source_target_pairs={{0,4},{1,5},{2,6},{3,7},{4,0},{5,1},{6,2},{7,3},{8,12},{9,13},{10,... | collective-permute-start | bytes 1327112 | tf_op jit(solution)/shard_map/ppermute | solution.py:86
  101.3 41.6 %collective-permute-start.4 = (f32[1728,64]{0,1:T(8,128)S(1)}, f32[1728,64]{0,1:T(8,128)S(1)}, u32[]{:S(2)}, u32[]{:S(2)}) collective-permute-start(f32[1728,64]{0,1:T(8,128)S(1)} %add.78), channel_id=1, source_target_pairs={{0,8},{1,9},{2,10},{3,11},{4,12},{5,13},{6,14},{7,15},{8,0},{9,1},... | collective-permute-start | bytes 1327112 | tf_op jit(solution)/shard_map/ppermute | solution.py:86
  212.1 14.3 %copy-start.1 = (bf16[1,108,1728]{2,1,0:T(8,128)(2,1)S(1)}, bf16[1,108,1728]{2,1,0:T(8,128)(2,1)}, u32[]{:S(2)}) copy-start(bf16[1,108,1728]{2,1,0:T(8,128)(2,1)} %param.12) | copy-start | bytes 1119748
Sparse Core Ops, SparseCore 0:
  11.4 180.4 all-gather.2
where the time goes:
time: 240 us; the launch traced here: 239 us
  waiting for transfers between devices  142 us (59%)
  other arithmetic  38.3 us (16%)
  local copies, waits for them, and re-layouts  24.1 us (10%)
  between operations  15.6 us (6%)
  matrix products  10.2 us (4%)
  starting transfers between devices  8.92 us (4%)
    ppermute x4, waiting for transfers between devices, doubling_sum(): lax.ppermute(value, axis, [(i, i ^ stride) for i in range(count)])  91.4 us
    all_gather x1, waiting for transfers between devices, shards(): gathered = lax.all_gather(a_factor[0], 'dp', axis=0, tiled=True)  48.4 us
    reduce_sum x1, other arithmetic, shards(): step_size = 1.0 / jnp.max(jnp.sum(jnp.abs(full_values), axis=1))  18.9 us
    mul x1, other arithmetic, shards(): step_size * full_values  14.3 us
    unnamed x37, local copies, waits for them, and re-layouts  8.38 us
    while x60, local copies, waits for them, and re-layouts  7.65 us
    ppermute x2, starting transfers between devices, shifted(): lax.ppermute(value, axis, [(source, source + steps) for source in range(f...  4.81 us
  transfers between devices with their start and end apart: 7, of which 7 were waited for; matrix products, arithmetic and copies ran while one was open for 12% of the time, Pallas kernels for 0%

commit v1 on v0

--- a/solution.py
+++ b/solution.py
@@ -92,7 +92,9 @@
     section_index = lax.axis_index("section")
     section_count = lax.axis_size("section")
     tick_count = MICRO + section_count - 1
-    gathered = lax.all_gather(a_factor[0], "dp", axis=0, tiled=True)
+    gathered = jnp.concatenate(
+        lax.all_to_all(jnp.stack([a_factor[0]] * lax.axis_size("dp")), "dp", 0, 0), axis=0
+    )
     inputs = acts[0, 0]
     pre_values = preacts[0, 0]
     upper_grads = top_grad[0]

time: 240 us -> 229 us (0.954); the launches traced: 239 us -> 225 us
  local copies, waits for them, and re-layouts: 24.1 us -> 45.9 us
  other arithmetic: 38.3 us -> 21 us
  waiting for transfers between devices: 142 us -> 126 us
  between operations: 15.6 us -> 2.19 us
  matrix products: 10.2 us -> 17.1 us
  starting transfers between devices: 8.92 us -> 12.8 us
    all_gather x1 -> x0, waiting for transfers between devices: 48.4 us -> none  [shards(): gathered = lax.all_gather(a_factor[0], 'dp', axis=0, tiled=True)]
    ppermute x4, waiting for transfers between devices: 91.4 us -> 124 us  [doubling_sum(): lax.ppermute(value, axis, [(i, i ^ stride) for i in range(count)])]
    reduce_sum x1, other arithmetic: 18.9 us -> 4.21 us  [shards(): step_size = 1.0 / jnp.max(jnp.sum(jnp.abs(full_values), axis=1))]
    mul x0 -> x1, local copies, waits for them, and re-layouts: none -> 11.6 us  [shards(): step_size * full_values]
    convert_element_type x0 -> x1, local copies, waits for them, and re-layouts: none -> 8.77 us  [shards(): (jnp.eye(order_full, dtype=jnp.float32) - step_size * full_values).astype...]
    all_to_all x0 -> x1, starting transfers between devices: none -> 6.82 us  [shards(): lax.all_to_all(jnp.stack([a_factor[0]] * lax.axis_size('dp')), 'dp', 0, 0)]
    dot_general x1, matrix products: 1.4 us -> 5.79 us  [shards(): jnp.dot(resid1, full_resid0, preferred_element_type=jnp.float32)]
    another operation x2 -> x3, local copies, waits for them, and re-layouts: 1.3 us -> 5.38 us  [the longest x1 4.07 us: shards(): jnp.stack([a_factor[0]] * lax.axis_size('dp'))]
  transfers between devices with their start and end apart: 7 -> 7, of which waited for: 7 -> 6; matrix products, arithmetic and copies ran while one was open for 12% -> 13% of each run, Pallas kernels for 0% -> 0%
where the time goes in v1:
time: 229 us; the launch traced here: 225 us
  waiting for transfers between devices  126 us (55%)
  local copies, waits for them, and re-layouts  45.9 us (20%)
  other arithmetic  21 us (9%)
  matrix products  17.1 us (7%)
  starting transfers between devices  12.8 us (6%)
    ppermute x4, waiting for transfers between devices, doubling_sum(): lax.ppermute(value, axis, [(i, i ^ stride) for i in range(count)])  124 us
    mul x1, other arithmetic, shards(): step_size * full_values  11.7 us
    mul x1, local copies, waits for them, and re-layouts, shards(): step_size * full_values  11.6 us
    convert_element_type x1, local copies, waits for them, and re-layouts, shards(): (jnp.eye(order_full, dtype=jnp.float32) - step_size * full_values).astype...  8.77 us
    while x60, local copies, waits for them, and re-layouts  7.65 us
    all_to_all x1, starting transfers between devices, shards(): lax.all_to_all(jnp.stack([a_factor[0]] * lax.axis_size('dp')), 'dp', 0, 0)  6.82 us
    unnamed x36, local copies, waits for them, and re-layouts  5.82 us
    dot_general x1, matrix products, shards(): jnp.dot(resid1, full_resid0, preferred_element_type=jnp.float32)  5.79 us
  transfers between devices with their start and end apart: 7, of which 6 were waited for; matrix products, arithmetic and copies ran while one was open for 13% of the time, Pallas kernels for 0%

profile of v1, /device:TPU:7, one launch (start us, length us, event | category | flops | bytes accessed | tf_op | source)
XLA Modules:
  0.0 225.4 jit_solution(13754976916206236490)
XLA Ops:
  0.6 4.1 %stack.367 = bf16[16,108,1728]{2,1,0:T(8,128)(2,1)} broadcast(bf16[108,1728]{1,0:T(8,128)(2,1)} %bitcast.353), dimensions={1,2} | broadcast | bytes 6345216 | tf_op jit(solution)/shard_map/stack | solution.py:96
  4.7 6.8 %all-to-all-start = ((bf16[16,108,1728]{2,1,0:T(8,128)(2,1)}), bf16[16,108,1728]{2,1,0:T(8,128)(2,1)}, u32[]{:S(2)}, u32[]{:S(2)}) async-start(bf16[16,108,1728]{2,1,0:T(8,128)(2,1)} %stack.367), calls=%async_computation | async-start | bytes 12845056 | tf_op jit(solution)/shard_map/all_to_all | solution.py:96
  12.0 0.9 copy.18
  16.3 2.1 reshape.110
  18.5 0.6 broadcast.64
  19.1 0.7 broadcast.65
  19.8 25.0 %while.20 = (s32[]{:T(128)}, bf16[64,2,2,128]{3,2,1,0:T(2,128)(2,1)}, bf16[1,64,2,2,128]{4,3,2,1,0:T(2,128)(2,1)}, bf16[1,64,2,2,128]{4,3,2,1,0:T(2,128)(2,1)}, ...) while((s32[]{:T(128)}, ...), condition=%wide.region_1.2_spmd.clone, body=%wide.region_0.1_spmd.clone.sunk | while | flops 113475592 | bytes 10772739 | solution.py:131
  19.8 3.1 %collective-permute-start = (bf16[64,2,2,128]{3,2,1,0:T(2,128)(2,1)}, bf16[64,2,2,128]{3,2,1,0:T(2,128)(2,1)S(1)}, u32[]{:S(2)}, u32[]{:S(2)}) collective-permute-start(bf16[64,2,2,128]{3,2,1,0:T(2,128)(2,1)} %get-tuple-element.364), channel_id=1, source_target_pairs={{16,0},{17,1},{18,2},{19,3},{20,4},{21,5},{22,6},{23,7},{24,8},{25... | collective-permute-start | bytes 196616 | tf_op jit(solution)/shard_map/while/body/eval_jaxpr/ppermute | solution.py:13
  23.0 1.1 collective-permute-done
  24.0 1.7 fusion.176
  29.1 0.7 reshape.117
  29.8 1.5 fusion.203
  31.3 0.6 reshape.118
  32.7 2.2 collective-permute-start
  35.0 1.1 collective-permute-done
  36.1 1.7 fusion.176
  41.1 0.7 reshape.117
  41.9 1.5 fusion.203
  44.8 0.9 reshape_squeeze.7
  45.6 2.1 fusion.133
  48.1 44.9 %collective-permute-done.1 = f32[1728,64]{0,1:T(8,128)S(1)} collective-permute-done((f32[1728,64]{0,1:T(8,128)S(1)}, f32[1728,64]{0,1:T(8,128)S(1)}, u32[]{:S(2)}, u32[]{:S(2)}) %collective-permute-start.1) | collective-permute-done | bytes 442400 | tf_op jit(solution)/shard_map/ppermute | solution.py:86
  93.2 16.7 %collective-permute-done.2 = f32[1728,64]{0,1:T(8,128)S(1)} collective-permute-done((f32[1728,64]{0,1:T(8,128)S(1)}, f32[1728,64]{0,1:T(8,128)S(1)}, u32[]{:S(2)}, u32[]{:S(2)}) %collective-permute-start.2) | collective-permute-done | bytes 442400 | tf_op jit(solution)/shard_map/ppermute | solution.py:86
  111.5 35.2 %collective-permute-done.3 = f32[1728,64]{0,1:T(8,128)S(1)} collective-permute-done((f32[1728,64]{0,1:T(8,128)S(1)}, f32[1728,64]{0,1:T(8,128)S(1)}, u32[]{:S(2)}, u32[]{:S(2)}) %collective-permute-start.3) | collective-permute-done | bytes 442400 | tf_op jit(solution)/shard_map/ppermute | solution.py:86
  147.1 27.2 %collective-permute-done.4 = f32[1728,64]{0,1:T(8,128)S(1)} collective-permute-done((f32[1728,64]{0,1:T(8,128)S(1)}, f32[1728,64]{0,1:T(8,128)S(1)}, u32[]{:S(2)}, u32[]{:S(2)}) %collective-permute-start.4) | collective-permute-done | bytes 442400 | tf_op jit(solution)/shard_map/ppermute | solution.py:86
  174.9 4.2 %fusion.54 = f32[16,108]{1,0:T(8,128)S(1)} fusion(bf16[16,108,1728]{2,1,0:T(8,128)(2,1)} %all-to-all-done), kind=kLoop, calls=%fused_computation.89 | loop fusion | flops 8956224 | bytes 5978880 | tf_op jit(solution)/shard_map/reduce_sum | solution.py:140
  180.4 11.7 %convert_multiply_fusion = (f32[16,108,1728]{2,1,0:T(8,128)}, bf16[16,108,1728]{2,1,0:T(8,128)(2,1)}) fusion(bf16[16,108,1728]{2,1,0:T(8,128)(2,1)} %all-to-all-done, f32[]{:T(128)S(6)} %div.12, s32[16,108]{1,0:T(8,128)S(1)} %multiply_add_fusion), kind=kLoop, calls=%fused_computation.87 | loop fusion | flops 17915904 | bytes 23894788 | tf_op jit(solution)/shard_map/mul | solution.py:141
  192.1 8.8 %convert_element_type.127 = bf16[1728,1728]{1,0:T(8,128)(2,1)} reshape(bf16[16,108,1728]{2,1,0:T(8,128)(2,1)} %get-tuple-element.292) | data formatting | bytes 11943936 | tf_op jit(solution)/shard_map/convert_element_type | solution.py:141
  200.8 11.6 %mul.52 = f32[1728,1728]{1,0:T(8,128)} reshape(f32[16,108,1728]{2,1,0:T(8,128)} %get-tuple-element.291) | data formatting | bytes 23887872 | tf_op jit(solution)/shard_map/mul | solution.py:141
  212.5 3.8 %convolution_convert_fusion.1 = bf16[108,1728]{1,0:T(8,128)(2,1)S(1)} fusion(bf16[1728,1728]{1,0:T(8,128)(2,1)} %convert_element_type.127, bf16[1,108,1728]{2,1,0:T(8,128)(2,1)S(1)} %copy-done.1, f32[]{:T(128)S(6)} %div.12, s32[108]{0:T(128)S(1)} %iota_add_fusion), kind=kOutput, calls=%fused_computation.123 | convolution fusion | flops 646278912 | bytes 6718900 | tf_op jit(solution)/shard_map/dot_general | solution.py:146
  216.3 5.8 %fusion.57 = f32[108,1728]{1,0:T(8,128)S(1)} fusion(bf16[108,1728]{1,0:T(8,128)(2,1)S(1)} %convolution_convert_fusion.1, f32[1728,1728]{1,0:T(8,128)} %mul.52, s32[108]{0:T(128)S(1)} %iota_add_fusion, f32[]{:T(128)S(6)} %div.12, bf16[1,108,1728]{2,1,0:T(8,128)(2,1)S(1)} %copy-done.1), kind=kOutput, calls=%fused_computation.122 | convolution fusion | flops 659155968 | bytes 13437364 | tf_op jit(solution)/shard_map/dot_general | solution.py:147
  222.1 1.6 convolution_bitcast_fusion
  223.7 1.7 copy.17
  (120 shorter events, 15.5 us)
Async XLA Ops:
  4.7 6.9 %copy-start.4 = (bf16[1,64,1728]{2,1,0:T(8,128)(2,1)S(1)}, bf16[1,64,1728]{2,1,0:T(8,128)(2,1)}, u32[]{:S(2)}) copy-start(bf16[1,64,1728]{2,1,0:T(8,128)(2,1)} %param.11) | copy-start | bytes 663556
  4.7 170.2 %all-to-all-start = ((bf16[16,108,1728]{2,1,0:T(8,128)(2,1)}), bf16[16,108,1728]{2,1,0:T(8,128)(2,1)}, u32[]{:S(2)}, u32[]{:S(2)}) async-start(bf16[16,108,1728]{2,1,0:T(8,128)(2,1)} %stack.367), calls=%async_computation | async-start | bytes 12845056 | tf_op jit(solution)/shard_map/all_to_all | solution.py:96
  11.5 1.5 copy-start
  19.8 4.2 %collective-permute-start = (bf16[64,2,2,128]{3,2,1,0:T(2,128)(2,1)}, bf16[64,2,2,128]{3,2,1,0:T(2,128)(2,1)S(1)}, u32[]{:S(2)}, u32[]{:S(2)}) collective-permute-start(bf16[64,2,2,128]{3,2,1,0:T(2,128)(2,1)} %get-tuple-element.364), channel_id=1, source_target_pairs={{16,0},{17,1},{18,2},{19,3},{20,4},{21,5},{22,6},{23,7},{24,8},{25... | collective-permute-start | bytes 196616 | tf_op jit(solution)/shard_map/while/body/eval_jaxpr/ppermute | solution.py:13
  29.8 2.2 copy-start.2
  32.1 0.6 copy-start.3
  32.7 3.3 %collective-permute-start = (bf16[64,2,2,128]{3,2,1,0:T(2,128)(2,1)}, bf16[64,2,2,128]{3,2,1,0:T(2,128)(2,1)S(1)}, u32[]{:S(2)}, u32[]{:S(2)}) collective-permute-start(bf16[64,2,2,128]{3,2,1,0:T(2,128)(2,1)} %get-tuple-element.364), channel_id=1, source_target_pairs={{16,0},{17,1},{18,2},{19,3},{20,4},{21,5},{22,6},{23,7},{24,8},{25... | collective-permute-start | bytes 196616 | tf_op jit(solution)/shard_map/while/body/eval_jaxpr/ppermute | solution.py:13
  41.8 2.2 copy-start.2
  44.1 0.6 copy-start.3
  47.8 62.3 %copy-start.5 = (bf16[1,64,64]{2,1,0:T(8,128)(2,1)S(1)}, bf16[1,64,64]{2,1,0:T(8,128)(2,1)}, u32[]{:S(2)}) copy-start(bf16[1,64,64]{2,1,0:T(8,128)(2,1)} %param.13) | copy-start | bytes 24580
  47.8 45.3 %collective-permute-start.1 = (f32[1728,64]{0,1:T(8,128)S(1)}, f32[1728,64]{0,1:T(8,128)S(1)}, u32[]{:S(2)}, u32[]{:S(2)}) collective-permute-start(f32[1728,64]{0,1:T(8,128)S(1)} %fusion.133), channel_id=1, source_target_pairs={{0,1},{1,0},{2,3},{3,2},{4,5},{5,4},{6,7},{7,6},{8,9},{9,8},{10,11... | collective-permute-start | bytes 1327112 | tf_op jit(solution)/shard_map/ppermute | solution.py:86
  93.1 16.8 %collective-permute-start.2 = (f32[1728,64]{0,1:T(8,128)S(1)}, f32[1728,64]{0,1:T(8,128)S(1)}, u32[]{:S(2)}, u32[]{:S(2)}) collective-permute-start(f32[1728,64]{0,1:T(8,128)S(1)} %add.80), channel_id=1, source_target_pairs={{0,2},{1,3},{2,0},{3,1},{4,6},{5,7},{6,4},{7,5},{8,10},{9,11},{10,... | collective-permute-start | bytes 1327112 | tf_op jit(solution)/shard_map/ppermute | solution.py:86
  110.0 36.7 %collective-permute-start.3 = (f32[1728,64]{0,1:T(8,128)S(1)}, f32[1728,64]{0,1:T(8,128)S(1)}, u32[]{:S(2)}, u32[]{:S(2)}) collective-permute-start(f32[1728,64]{0,1:T(8,128)S(1)} %add.81), channel_id=1, source_target_pairs={{0,4},{1,5},{2,6},{3,7},{4,0},{5,1},{6,2},{7,3},{8,12},{9,13},{10,... | collective-permute-start | bytes 1327112 | tf_op jit(solution)/shard_map/ppermute | solution.py:86
  146.8 27.5 %collective-permute-start.4 = (f32[1728,64]{0,1:T(8,128)S(1)}, f32[1728,64]{0,1:T(8,128)S(1)}, u32[]{:S(2)}, u32[]{:S(2)}) collective-permute-start(f32[1728,64]{0,1:T(8,128)S(1)} %add.82), channel_id=1, source_target_pairs={{0,8},{1,9},{2,10},{3,11},{4,12},{5,13},{6,14},{7,15},{8,0},{9,1},... | collective-permute-start | bytes 1327112 | tf_op jit(solution)/shard_map/ppermute | solution.py:86
  200.8 11.6 %copy-start.1 = (bf16[1,108,1728]{2,1,0:T(8,128)(2,1)S(1)}, bf16[1,108,1728]{2,1,0:T(8,128)(2,1)}, u32[]{:S(2)}) copy-start(bf16[1,108,1728]{2,1,0:T(8,128)(2,1)} %param.12) | copy-start | bytes 1119748
